TPU v7x, 32 devices: a whole 2x2x4 slice. The times are simulated.
32 devices in a mesh: seq: 4 (over z), ch: 8 (over y, x, core).
Axes of the slice: x: 2, y: 2, z: 4, core: 2. Of those that a mesh axis runs over, the one named last changes fastest.
Arguments:
- inputs: bfloat16 [1024, 8192], P('seq', 'ch'), may hold values from -6 to 6
- w_in: bfloat16 [3, 8192, 8192], P(None, 'seq', 'ch'), may hold values from -0.0625 to 0.0625
- short_filter: float32 [3, 3, 8192], P(None, None, 'ch'), may hold values from -3 to 3
- rates: float32 [16, 8192], P(None, 'ch'), may hold values from 9.765625e-05 to 0.05
- residues: float32 [16, 8192], P(None, 'ch'), may hold values from -3 to 3
- skip: float32 [8192], P('ch'), may hold values from -3 to 3
Outputs:
- gated: bfloat16 [1024, 8192], P('seq', 'ch')
All inputs are finite; a program needn't handle non-finite values.
Results may differ from a plain program's by a relative error of at most 0.0065.
Values may be sent and summed in bfloat16 or wider, within the bound.
No kernel may reach another device: no remote copies, remote signals or barrier semaphores. Data moves between devices by JAX's collectives and lax.ppermute only.
A program may use at most 128 MiB of HBM per device.

v0:
```python
import jax
import jax.numpy as jnp
from jax import lax
from jax.sharding import PartitionSpec as P

TAPS = 3


def passed_along(block, axis, distance):
    devices = range(lax.axis_size(axis))
    route = [(i - distance, i) for i in devices if i - distance in devices]
    return lax.ppermute(block, axis, route)


def carried_in(end_state, decay, axis):
    total = lax.axis_size(axis)
    state = jnp.zeros_like(end_state)
    for distance in range(total - 1, 0, -1):
        state = state * decay + passed_along(end_state, axis, distance)
    return state


def project(inputs, w_in):
    tok_rows, local = inputs.shape
    n_seq = lax.axis_size("seq")
    n_ch = lax.axis_size("ch")
    share = tok_rows // n_ch
    pieces = lax.all_to_all(inputs.reshape(n_ch, share, local), "ch", 0, 0, tiled=True)
    pieces = pieces.transpose(1, 0, 2).reshape(share, n_seq, n_ch * local // n_seq)
    rows = lax.all_to_all(pieces, "seq", 1, 0, tiled=True)
    rows = rows.reshape(n_seq, share, rows.shape[-1])
    block = lax.all_gather(rows, "ch", axis=1, tiled=True)
    block = block.reshape(n_seq * tok_rows, block.shape[-1])
    partial = jnp.einsum("td,kdc->ktc", block, w_in, preferred_element_type=jnp.float32)
    return lax.psum_scatter(partial, "seq", scatter_dimension=1, tiled=True)


def per_device(inputs, w_in, short_filter, rates, residues, skip):
    tok_rows = inputs.shape[0]
    width = w_in.shape[2]
    modes = rates.shape[0]
    proj = project(inputs, w_in).astype(jnp.bfloat16)
    prior = passed_along(proj[:, tok_rows - (TAPS - 1) :, :], "seq", 1)
    padded = jnp.concatenate([prior, proj], axis=1).astype(jnp.float32)
    mixed = jnp.zeros((3, tok_rows, width), jnp.float32)
    for j in range(TAPS):
        mixed = (
            mixed
            + short_filter[:, j, None, :] * padded[:, TAPS - 1 - j : TAPS - 1 - j + tok_rows, :]
        )
    query, key, value = (mixed[0], mixed[1], mixed[2])
    drive = key * value
    position = jnp.arange(tok_rows, dtype=jnp.float32)
    scaled = residues * jnp.sqrt(1.0 - jnp.exp(-2.0 * rates))
    end_powers = jnp.exp(-rates[None, :, :] * (tok_rows - 1.0 - position)[:, None, None])
    end_state = jnp.sum(end_powers * drive[:, None, :], axis=0)
    block_decay = jnp.exp(-rates * tok_rows)
    entering = carried_in(end_state, block_decay, "seq")
    start_powers = jnp.exp(-rates[None, :, :] * (position + 1.0)[:, None, None])
    cross = jnp.sum(start_powers * (scaled * entering)[None, :, :], axis=1)
    center = (tok_rows - 1.0) / 2.0
    offset = (position - center)[:, None, None]
    rising = jnp.exp(rates[None, :, :] * offset) * drive[:, None, :]
    offsets = jnp.arange(tok_rows, dtype=jnp.int32)
    lower = (offsets[:, None] >= offsets[None, :]).astype(jnp.float32)
    prefix = jnp.dot(
        lower, rising.reshape(tok_rows, modes * width), precision=lax.Precision.HIGHEST
    )
    prefix = prefix.reshape(tok_rows, modes, width)
    falling = jnp.exp(-rates[None, :, :] * offset) * scaled[None, :, :]
    local = jnp.sum(falling * prefix, axis=1)
    return (query * (local + cross + skip[None, :] * drive)).astype(jnp.bfloat16)


def solution(mesh):
    in_specs = (
        P("seq", "ch"),
        P(None, "seq", "ch"),
        P(None, None, "ch"),
        P(None, "ch"),
        P(None, "ch"),
        P("ch"),
    )
    out_specs = P("seq", "ch")
    return jax.shard_map(
        per_device, mesh=mesh, in_specs=in_specs, out_specs=out_specs, check_vma=False
    )
```

profile of v0, /device:TPU:0, one launch (start us, length us, event | category | flops | bytes accessed | tf_op | source)
XLA Modules:
  0.0 379.0 jit_solution(15950338442145141932)
XLA Ops:
  6.5 14.9 %all_to_all.20 = bf16[8,32,1024]{2,1,0:T(8,128)(2,1)S(1)} all-to-all(bf16[8,32,1024]{2,1,0:T(8,128)(2,1)} %bitcast.45), channel_id=1, replica_groups=mesh['seq'=4,'ch'=8] {'ch'}, dimensions={0} | all-to-all | bytes 1048576 | tf_op jit(solution)/shard_map/all_to_all | solution.py:28
  22.4 18.6 %all_to_all.21 = bf16[32,4,2048]{2,0,1:T(8,128)(2,1)S(1)} all-to-all(bf16[32,4,2048]{2,0,1:T(8,128)(2,1)S(1)} %copy.17), channel_id=1, replica_groups=mesh['seq'=4,'ch'=8] {'seq'}, dimensions={1} | all-to-all | bytes 1048576 | tf_op jit(solution)/shard_map/all_to_all | solution.py:30
  41.0 1.2 copy.18
  42.3 34.5 %all-gather.3.cloned.1.call-done = bf16[4,256,1,2048]{3,0,2,1:T(4,128)(2,1)} async-done(((bf16[4,32,1,2048]{3,0,2,1:T(4,128)(2,1)}), bf16[4,256,1,2048]{3,0,2,1:T(4,128)(2,1)}) %all-gather.3.cloned.1.call-update) | async-done | bytes 4194320 | tf_op jit(solution)/shard_map/all_gather | solution.py:32
  76.8 4.5 %copy.19 = bf16[4,256,1,2048]{3,1,0,2:T(8,128)(2,1)S(1)} copy(bf16[4,256,1,2048]{3,0,2,1:T(4,128)(2,1)} %all-gather.3.cloned.1.call-done) | data formatting | bytes 8388608 | tf_op jit(solution)/shard_map/all_gather | solution.py:32
  81.3 17.8 %convolution_bitcast_fusion = f32[3,1024,1024]{1,2,0:T(8,128)} fusion(bf16[3,2048,1024]{2,1,0:T(8,128)(2,1)} %param.7, bf16[1024,2048,1]{1,0,2:T(8,128)(2,1)S(1)} %bitcast.41), kind=kOutput, calls=%fused_computation.4 | convolution fusion | flops 12884901888 | bytes 29360128 | tf_op jit(solution)/shard_map/td,kdc->ktc/dot_general | solution.py:34
  100.0 211.2 %reduce-scatter.2.cloned.1.call-done = f32[3,256,1024]{1,2,0:T(8,128)} async-done(((f32[3,1024,1024]{1,2,0:T(8,128)}), f32[3,256,1024]{1,2,0:T(8,128)}) %reduce-scatter.2.cloned.1.call-update) | async-done | bytes 3145744 | tf_op jit(solution)/shard_map/reduce_scatter | solution.py:35
  311.2 2.0 convert_element_type.10
  313.8 3.6 collective-permute-start
  317.5 1.1 collective-permute-done
  320.0 3.2 fusion
  323.2 1.1 fusion.2
  324.3 2.6 copy.23
  326.9 4.2 %multiply_reduce_fusion.1 = f32[16,1024]{1,0:T(8,128)S(1)} fusion(f32[256]{0:T(256)S(1)} %iota_subtract_fusion, f32[256,1024]{1,0:T(8,128)} %copy.23, f32[16,1024]{1,0:T(8,128)S(1)} %neg.3), kind=kLoop, calls=%fused_computation.2 | loop fusion | flops 12566528 | bytes 1180672 | tf_op jit(solution)/shard_map/reduce_sum | solution.py:56
  331.0 5.8 %collective-permute-start.1 = (f32[16,1024]{1,0:T(8,128)S(1)}, f32[16,1024]{1,0:T(8,128)S(1)}, u32[]{:S(2)}, u32[]{:S(2)}) collective-permute-start(f32[16,1024]{1,0:T(8,128)S(1)} %multiply_reduce_fusion.1), channel_id=1, source_target_pairs={{0,24},{1,25},{2,26},{3,27},{4,28},{5,29},{6,30},{7,31}} | collective-permute-start | bytes 196616 | tf_op jit(solution)/shard_map/ppermute | solution.py:12
  336.9 1.3 collective-permute-start.2
  338.2 2.5 collective-permute-start.3
  340.7 3.8 bitcast_multiply_fusion
  344.6 14.1 %multiply_reduce_fusion.2 = f32[256,1024]{1,0:T(8,128)} fusion(f32[16,1024,256]{2,1,0:T(8,128)S(1)} %bitcast.40, f32[16,1024]{1,0:T(8,128)S(1)} %get-tuple-element.6, f32[256]{0:T(256)S(1)} %iota_add_fusion.1, f32[16,1024]{1,0:T(8,128)S(1)} %neg.3), kind=kOutput, calls=%fused_computation.3 | convolution fusion | flops 12901482496 | bytes 17957888 | tf_op jit(solution)/shard_map/dot_general | solution.py:66
  358.6 2.5 copy.25
  361.2 3.8 multiply_reduce_fusion
  364.9 2.6 copy.26
  367.5 2.6 fusion.4
  370.1 2.0 copy.27
  (31 shorter events, 4.0 us)
Async XLA Ops:
  6.5 70.3 %all-gather.3.cloned.1.call-start = ((), (), s32[]{:S(2)}) async-start(), calls=%async_computation.4 | async-start | bytes 4718592 | tf_op jit(solution)/shard_map/all_gather | solution.py:32
  42.3 268.9 %reduce-scatter.2.cloned.1.call-start = ((), (), s32[]{:S(2)}) async-start(), calls=%async_computation.3 | async-start | bytes 15728640 | tf_op jit(solution)/shard_map/reduce_scatter | solution.py:35
  99.1 0.8 copy-start.2
  99.1 218.3 %copy-start = (f32[16,1024]{1,0:T(8,128)S(1)}, f32[16,1024]{1,0:T(8,128)}, u32[]{:S(2)}) copy-start(f32[16,1024]{1,0:T(8,128)} %param.9) | copy-start | bytes 196612
  313.8 4.8 %collective-permute-start = (bf16[3,2,1024]{2,1,0:T(2,128)(2,1)S(1)}, bf16[3,2,1024]{2,1,0:T(2,128)(2,1)S(1)}, u32[]{:S(2)}, u32[]{:S(2)}) collective-permute-start(bf16[3,2,1024]{2,1,0:T(2,128)(2,1)S(1)} %copy.21), channel_id=1, source_target_pairs={{0,8},{8,16},{16,24},{1,9},{9,17},{17,25},{2,10},{10,18},{18,26},{... | collective-permute-start | bytes 36872 | tf_op jit(solution)/shard_map/ppermute | solution.py:12
  326.9 17.6 %copy-start.1 = (f32[16,1024]{1,0:T(8,128)S(1)}, f32[16,1024]{1,0:T(8,128)}, u32[]{:S(2)}) copy-start(f32[16,1024]{1,0:T(8,128)} %param.10) | copy-start | bytes 196612
  331.0 13.4 %collective-permute-start.1 = (f32[16,1024]{1,0:T(8,128)S(1)}, f32[16,1024]{1,0:T(8,128)S(1)}, u32[]{:S(2)}, u32[]{:S(2)}) collective-permute-start(f32[16,1024]{1,0:T(8,128)S(1)} %multiply_reduce_fusion.1), channel_id=1, source_target_pairs={{0,24},{1,25},{2,26},{3,27},{4,28},{5,29},{6,30},{7,31}} | collective-permute-start | bytes 196616 | tf_op jit(solution)/shard_map/ppermute | solution.py:12
  336.9 7.6 %collective-permute-start.2 = (f32[16,1024]{1,0:T(8,128)S(1)}, f32[16,1024]{1,0:T(8,128)S(1)}, u32[]{:S(2)}, u32[]{:S(2)}) collective-permute-start(f32[16,1024]{1,0:T(8,128)S(1)} %multiply_reduce_fusion.1), channel_id=1, source_target_pairs={{0,16},{8,24},{1,17},{9,25},{2,18},{10,26},{3,19},{11,27},{4,20},{... | collective-permute-start | bytes 196616 | tf_op jit(solution)/shard_map/ppermute | solution.py:12
  338.2 6.3 %collective-permute-start.3 = (f32[16,1024]{1,0:T(8,128)S(1)}, f32[16,1024]{1,0:T(8,128)S(1)}, u32[]{:S(2)}, u32[]{:S(2)}) collective-permute-start(f32[16,1024]{1,0:T(8,128)S(1)} %multiply_reduce_fusion.1), channel_id=1, source_target_pairs={{0,8},{8,16},{16,24},{1,9},{9,17},{17,25},{2,10},{10,18},{18,26},{... | collective-permute-start | bytes 196616 | tf_op jit(solution)/shard_map/ppermute | solution.py:12
  344.6 23.0 %copy-start.3 = (f32[1024]{0:T(1024)S(1)}, f32[1024]{0:T(1024)}, u32[]{:S(2)}) copy-start(f32[1024]{0:T(1024)} %param.11) | copy-start | bytes 12292
Sparse Core Ops, SparseCore 0:
  42.4 34.4 all-gather.2
  99.3 211.8 reduce-scatter.1
where the time goes:
time: 380 us; the launch traced here: 379 us
  waiting for transfers between devices  247 us (65%)
  blocking collectives  33.5 us (9%)
  matrix products  31.9 us (8%)
  other arithmetic  21.7 us (6%)
  local copies, waits for them, and re-layouts  18.2 us (5%)
  between operations  13.6 us (4%)
  starting transfers between devices  13.2 us (3%)
    reduce_scatter x1, waiting for transfers between devices, project(): return lax.psum_scatter(partial, 'seq', scatter_dimension=1, tiled=True)  211 us
    all_gather x1, waiting for transfers between devices, project(): block = lax.all_gather(rows, 'ch', axis=1, tiled=True)  34.5 us
    all_to_all x1, blocking collectives, project(): rows = lax.all_to_all(pieces, 'seq', 1, 0, tiled=True)  18.6 us
    dot_general x1, matrix products, project(): jnp.einsum('td,kdc->ktc', block, w_in, preferred_element_type=jnp.float32)  17.8 us
    all_to_all x1, blocking collectives, project(): lax.all_to_all(inputs.reshape(n_ch, share, local), 'ch', 0, 0, tiled=True)  14.9 us
    dot_general x1, matrix products, per_device(): jnp.dot(lower, rising.reshape(tok_rows, modes * width), precision=lax.Pre...  14.1 us
    ppermute x4, starting transfers between devices, passed_along(): return lax.ppermute(block, axis, route)  13.2 us
  transfers between devices with their start and end apart: 6, of which 3 were waited for; matrix products, arithmetic and copies ran while one was open for 1% of the time, Pallas kernels for 0%

commit v1 on v0

--- a/solution.py
+++ b/solution.py
@@ -27,7 +27,10 @@
     share = tok_rows // n_ch
     pieces = lax.all_to_all(inputs.reshape(n_ch, share, local), "ch", 0, 0, tiled=True)
     pieces = pieces.transpose(1, 0, 2).reshape(share, n_seq, n_ch * local // n_seq)
-    rows = lax.all_to_all(pieces, "seq", 1, 0, tiled=True)
+    rows = jnp.concatenate(
+        lax.all_to_all(jnp.stack(jnp.split(pieces, lax.axis_size("seq"), axis=1)), "seq", 0, 0),
+        axis=0,
+    )
     rows = rows.reshape(n_seq, share, rows.shape[-1])
     block = lax.all_gather(rows, "ch", axis=1, tiled=True)
     block = block.reshape(n_seq * tok_rows, block.shape[-1])

time: 380 us -> 364 us (0.958)
  local copies, waits for them, and re-layouts: 18.2 us -> 6.13 us
  other arithmetic: 21.7 us -> 16.5 us
    reduce_sum x2 -> x0, local copies, waits for them, and re-layouts: 5.12 us -> none  [the longest x1 2.58 us: per_device(): cross = jnp.sum(start_powers * (scaled * entering)[None, :, :], axis=1)]
    all_gather x1 -> x0, local copies, waits for them, and re-layouts: 4.48 us -> none  [project(): block = lax.all_gather(rows, 'ch', axis=1, tiled=True)]
    unnamed x11 -> x20, local copies, waits for them, and re-layouts: 0.8 us -> 4.64 us
  transfers between devices with their start and end apart: 6 -> 6, of which waited for: 3 -> 3; matrix products, arithmetic and copies ran while one was open for 1% -> 2% of each run, Pallas kernels for 0% -> 0%
where the time goes in v1:
time: 364 us; the launch traced here: 363 us
  waiting for transfers between devices  247 us (68%)
  blocking collectives  33.6 us (9%)
  matrix products  33 us (9%)
  other arithmetic  16.5 us (5%)
  between operations  13.7 us (4%)
  starting transfers between devices  13.2 us (4%)
  local copies, waits for them, and re-layouts  6.13 us (2%)
    reduce_scatter x1, waiting for transfers between devices, project(): return lax.psum_scatter(partial, 'seq', scatter_dimension=1, tiled=True)  211 us
    all_gather x1, waiting for transfers between devices, project(): block = lax.all_gather(rows, 'ch', axis=1, tiled=True)  34.5 us
    dot_general x1, matrix products, project(): jnp.einsum('td,kdc->ktc', block, w_in, preferred_element_type=jnp.float32)  18.9 us
    all_to_all x1, blocking collectives, project(): lax.all_to_all(jnp.stack(jnp.split(pieces, lax.axis_size('seq'), axis=1))...  18.7 us
    all_to_all x1, blocking collectives, project(): lax.all_to_all(inputs.reshape(n_ch, share, local), 'ch', 0, 0, tiled=True)  14.9 us
    dot_general x1, matrix products, per_device(): jnp.dot(lower, rising.reshape(tok_rows, modes * width), precision=lax.Pre...  14 us
    ppermute x4, starting transfers between devices, passed_along(): return lax.ppermute(block, axis, route)  13.2 us
  transfers between devices with their start and end apart: 6, of which 3 were waited for; matrix products, arithmetic and copies ran while one was open for 2% of the time, Pallas kernels for 0%

profile of v1, /device:TPU:0, one launch (start us, length us, event | category | flops | bytes accessed | tf_op | source)
XLA Modules:
  0.0 363.2 jit_solution(11586986080674037661)
XLA Ops:
  6.5 14.9 %all_to_all.10 = bf16[8,32,1024]{2,1,0:T(8,128)(2,1)S(1)} all-to-all(bf16[8,32,1024]{2,1,0:T(8,128)(2,1)} %bitcast.48), channel_id=1, replica_groups=mesh['seq'=4,'ch'=8] {'ch'}, dimensions={0} | all-to-all | bytes 1048576 | tf_op jit(solution)/shard_map/all_to_all | solution.py:28
  21.4 0.3 copy.26
  21.7 0.4 reshape.44
  22.1 0.8 fusion.7
  23.3 18.7 %all_to_all.11 = bf16[4,32,1,2048]{3,1,2,0:T(8,128)(2,1)} all-to-all(bf16[4,32,1,2048]{3,1,2,0:T(8,128)(2,1)S(1)} %pad_maximum_fusion), channel_id=1, replica_groups=mesh['seq'=4,'ch'=8] {'seq'}, dimensions={0} | all-to-all | bytes 1048576 | tf_op jit(solution)/shard_map/all_to_all | solution.py:31
  42.1 34.5 %all-gather.3.cloned.1.call-done = bf16[4,256,1,2048]{3,1,2,0:T(8,128)(2,1)} async-done(((bf16[4,32,1,2048]{3,1,2,0:T(8,128)(2,1)}), bf16[4,256,1,2048]{3,1,2,0:T(8,128)(2,1)}) %all-gather.3.cloned.1.call-update) | async-done | bytes 4194320 | tf_op jit(solution)/shard_map/all_gather | solution.py:35
  76.6 18.9 %convolution_bitcast_fusion = f32[3,1024,1024]{2,1,0:T(8,128)} fusion(bf16[1024,2048,1]{1,0,2:T(8,128)(2,1)} %bitcast.51, bf16[3,2048,1024]{2,1,0:T(8,128)(2,1)} %param.7), kind=kOutput, calls=%fused_computation.4 | convolution fusion | flops 12884901888 | bytes 29360128 | tf_op jit(solution)/shard_map/td,kdc->ktc/dot_general | solution.py:37
  95.6 0.8 copy-done.5
  96.4 211.2 %reduce-scatter.2.cloned.1.call-done = f32[3,256,1024]{2,1,0:T(8,128)} async-done(((f32[3,1024,1024]{2,1,0:T(8,128)}), f32[3,256,1024]{2,1,0:T(8,128)}) %reduce-scatter.2.cloned.1.call-update) | async-done | bytes 3145744 | tf_op jit(solution)/shard_map/reduce_scatter | solution.py:38
  307.6 2.1 convert_element_type.10
  309.7 3.4 collective-permute-start
  313.2 1.3 collective-permute-done
  314.5 0.5 maximum_convert_fusion
  315.0 0.9 fusion
  316.1 1.0 copy-done
  317.1 3.5 multiply_reduce_fusion.1
  320.6 4.4 %collective-permute-start.3 = (f32[16,1024]{1,0:T(8,128)}, f32[16,1024]{1,0:T(8,128)S(1)}, u32[]{:S(2)}, u32[]{:S(2)}) collective-permute-start(f32[16,1024]{1,0:T(8,128)} %multiply_reduce_fusion.1), channel_id=1, source_target_pairs={{0,8},{8,16},{16,24},{1,9},{9,17},{17,25},{2,10},{10,18},{18,26},{... | collective-permute-start | bytes 196616 | tf_op jit(solution)/shard_map/ppermute | solution.py:12
  325.0 3.9 %collective-permute-start.2 = (f32[16,1024]{1,0:T(8,128)}, f32[16,1024]{1,0:T(8,128)S(1)}, u32[]{:S(2)}, u32[]{:S(2)}) collective-permute-start(f32[16,1024]{1,0:T(8,128)} %multiply_reduce_fusion.1), channel_id=1, source_target_pairs={{0,16},{8,24},{1,17},{9,25},{2,18},{10,26},{3,19},{11,27},{4,20},{... | collective-permute-start | bytes 196616 | tf_op jit(solution)/shard_map/ppermute | solution.py:12
  328.9 1.5 collective-permute-start.1
  330.4 2.6 copy.36
  333.0 3.8 %bitcast_multiply_fusion = f32[256,16384]{0,1:T(8,128)S(1)} fusion(f32[256,1024]{0,1:T(8,128)} %copy.36, f32[256]{0:T(256)S(1)} %iota_add_fusion.1, f32[16384]{0:T(1024)S(1)} %bitcast.49), kind=kLoop, calls=%fused_computation | loop fusion | flops 8388608 | bytes 17892352 | tf_op jit(solution)/shard_map/mul | solution.py:66
  336.9 14.0 %multiply_reduce_fusion.2 = f32[256,1024]{1,0:T(8,128)} fusion(f32[16,1024,256]{2,1,0:T(8,128)S(1)} %bitcast.45, f32[16,1024]{1,0:T(8,128)S(1)} %get-tuple-element.6, f32[256]{0:T(256)S(1)} %iota_add_fusion.1, f32[16,1024]{1,0:T(8,128)S(1)} %copy-done.4), kind=kOutput, calls=%fused_computation.3 | convolution fusion | flops 12901482496 | bytes 17957888 | tf_op jit(solution)/shard_map/dot_general | solution.py:69
  350.9 2.8 multiply_reduce_fusion
  353.7 2.6 fusion.4
  (33 shorter events, 0.8 us)
Async XLA Ops:
  6.5 70.1 %all-gather.3.cloned.1.call-start = ((), (), s32[]{:S(2)}) async-start(), calls=%async_computation.4 | async-start | bytes 4718592 | tf_op jit(solution)/shard_map/all_gather | solution.py:35
  42.0 265.5 %reduce-scatter.2.cloned.1.call-start = ((), (), s32[]{:S(2)}) async-start(), calls=%async_computation.3 | async-start | bytes 15728640 | tf_op jit(solution)/shard_map/reduce_scatter | solution.py:38
  95.5 0.8 copy-start.5
  95.5 217.6 %copy-start.1 = (f32[16,1024]{1,0:T(8,128)S(1)}, f32[16,1024]{1,0:T(8,128)}, u32[]{:S(2)}) copy-start(f32[16,1024]{1,0:T(8,128)} %param.9) | copy-start | bytes 196612
  309.7 4.8 %collective-permute-start = (bf16[3,2,1024]{2,1,0:T(2,128)(2,1)S(1)}, bf16[3,2,1024]{2,1,0:T(2,128)(2,1)S(1)}, u32[]{:S(2)}, u32[]{:S(2)}) collective-permute-start(bf16[3,2,1024]{2,1,0:T(2,128)(2,1)S(1)} %slice.40), channel_id=1, source_target_pairs={{0,8},{8,16},{16,24},{1,9},{9,17},{17,25},{2,10},{10,18},{18,26},{... | collective-permute-start | bytes 36872 | tf_op jit(solution)/shard_map/ppermute | solution.py:12
  313.2 7.4 %copy-start.3 = (f32[16,1024]{1,0:T(8,128)}, f32[16,1024]{1,0:T(8,128)S(1)}, u32[]{:S(2)}) copy-start(f32[16,1024]{1,0:T(8,128)S(1)} %neg.3) | copy-start | bytes 196612
  316.1 1.0 copy-start
  317.1 19.7 %copy-start.2 = (f32[16,1024]{1,0:T(8,128)S(1)}, f32[16,1024]{1,0:T(8,128)}, u32[]{:S(2)}) copy-start(f32[16,1024]{1,0:T(8,128)} %param.10) | copy-start | bytes 196612
  320.6 16.2 %collective-permute-start.3 = (f32[16,1024]{1,0:T(8,128)}, f32[16,1024]{1,0:T(8,128)S(1)}, u32[]{:S(2)}, u32[]{:S(2)}) collective-permute-start(f32[16,1024]{1,0:T(8,128)} %multiply_reduce_fusion.1), channel_id=1, source_target_pairs={{0,8},{8,16},{16,24},{1,9},{9,17},{17,25},{2,10},{10,18},{18,26},{... | collective-permute-start | bytes 196616 | tf_op jit(solution)/shard_map/ppermute | solution.py:12
  325.0 11.7 %collective-permute-start.2 = (f32[16,1024]{1,0:T(8,128)}, f32[16,1024]{1,0:T(8,128)S(1)}, u32[]{:S(2)}, u32[]{:S(2)}) collective-permute-start(f32[16,1024]{1,0:T(8,128)} %multiply_reduce_fusion.1), channel_id=1, source_target_pairs={{0,16},{8,24},{1,17},{9,25},{2,18},{10,26},{3,19},{11,27},{4,20},{... | collective-permute-start | bytes 196616 | tf_op jit(solution)/shard_map/ppermute | solution.py:12
  328.9 7.9 %collective-permute-start.1 = (f32[16,1024]{1,0:T(8,128)}, f32[16,1024]{1,0:T(8,128)S(1)}, u32[]{:S(2)}, u32[]{:S(2)}) collective-permute-start(f32[16,1024]{1,0:T(8,128)} %multiply_reduce_fusion.1), channel_id=1, source_target_pairs={{0,24},{1,25},{2,26},{3,27},{4,28},{5,29},{6,30},{7,31}} | collective-permute-start | bytes 196616 | tf_op jit(solution)/shard_map/ppermute | solution.py:12
  333.0 3.9 %copy-start.4 = (f32[16,1024]{1,0:T(8,128)S(1)}, f32[16,1024]{1,0:T(8,128)}, u32[]{:S(2)}) copy-start(f32[16,1024]{1,0:T(8,128)} %copy-done.3) | copy-start | bytes 196612
  336.9 16.8 %copy-start.6 = (f32[1024]{0:T(1024)S(1)}, f32[1024]{0:T(1024)}, u32[]{:S(2)}) copy-start(f32[1024]{0:T(1024)} %param.11) | copy-start | bytes 12292
Sparse Core Ops, SparseCore 0:
  42.2 34.4 all-gather.2
  95.7 211.8 reduce-scatter.1
